TPU v7x, 256 devices: a whole 4x4x8 slice. The times are simulated.
256 devices in a mesh: gx: 16 (over y_lo, z), gy: 4 (over y_hi, core), gz: 4 (over x).
Axes of the slice: x: 4, y: 4 (y_hi: 2, y_lo: 2; y = y_hi * 2 + y_lo), z: 8, core: 2. Of those that a mesh axis runs over, the one named last changes fastest.
Arguments:
- velocity: float32 [3, 64, 32, 1024], P(None, 'gx', 'gy', 'gz'), may hold values from -6 to 6
- stress: float32 [6, 64, 32, 1024], P(None, 'gx', 'gy', 'gz'), may hold values from -6 to 6
- buoyancy: float32 [64, 32, 1024], P('gx', 'gy', 'gz'), may hold values from 0.5 to 1
- lame_lambda: float32 [64, 32, 1024], P('gx', 'gy', 'gz'), may hold values from 0.5 to 1.5
- shear_modulus: float32 [64, 32, 1024], P('gx', 'gy', 'gz'), may hold values from 0.3 to 1
- slip_rate: bfloat16 [2048, 4096], P(('gx', 'gy', 'gz')), may hold values from 0 to 2
- taps: bfloat16 [512], replicated, may hold values from -0.25 to 0.25
- moment: float32 [6, 2048], P(None, ('gx', 'gy', 'gz')), may hold values from -6 to 6
- cells: int32 [3, 2048], replicated, may hold values from 0 to 511, as said below
- onsets: int32 [2048], P(('gx', 'gy', 'gz')), may hold values from 0 to 2624, as said below
Outputs:
- velocity_out: float32 [3, 64, 32, 1024], P(None, 'gx', 'gy', 'gz')
- stress_out: float32 [6, 64, 32, 1024], P(None, 'gx', 'gy', 'gz')
Inputs may be any that keep to these rules, and one draw needn't show every extreme that they name: `cells`: row 0 is below 64, row 1 is 15 or 16, row 2 is below 512. `onsets`: every subfault's frames lie inside its slip-rate function.
All inputs are finite; a program needn't handle non-finite values.
Results may differ from a plain program's by a relative error of at most 0.0003.
Values sent between devices are 32-bit elements; how exact they have to be, the bound alone decides.
No kernel may reach another device: no remote copies, remote signals or barrier semaphores. Data moves between devices by JAX's collectives and lax.ppermute only.
A program may use at most 64 MiB of HBM per device.

v0:
```python
import jax
import jax.numpy as jnp
from jax import lax
from jax.sharding import PartitionSpec as P

TAPS = 512
HOP = 64
STEPS = 16
STEP_TIME = 0.25


def with_halo(block, sides, width):
    for axis, dim in sides:
        count = lax.axis_size(axis)
        forward = [(i, i + 1) for i in range(count - 1)]
        backward = [(target, source) for source, target in forward]
        low = lax.ppermute(
            lax.slice_in_dim(block, block.shape[dim] - width, None, axis=dim), axis, forward
        )
        high = lax.ppermute(lax.slice_in_dim(block, 0, width, axis=dim), axis, backward)
        block = jnp.concatenate([low, block, high], axis=dim)
    return block


def window(array, axis, offset):
    cuts = [slice(None)] * (array.ndim - 3)
    for dim in range(3):
        extent = array.shape[array.ndim - 3 + dim]
        if dim == axis:
            cuts.append(slice(1 + offset, extent - 1 + offset))
        else:
            cuts.append(slice(1, extent - 1))
    return array[tuple(cuts)]


def forward(array, axis):
    return window(array, axis, 1) - window(array, axis, 0)


def backward(array, axis):
    return window(array, axis, 0) - window(array, axis, -1)


def velocity_update(stress_pad, velocity, buoyancy):
    factor = STEP_TIME * buoyancy
    velocity_x = velocity[0] + factor * (
        forward(stress_pad[0], 0) + backward(stress_pad[3], 1) + backward(stress_pad[4], 2)
    )
    velocity_y = velocity[1] + factor * (
        backward(stress_pad[3], 0) + forward(stress_pad[1], 1) + backward(stress_pad[5], 2)
    )
    velocity_z = velocity[2] + factor * (
        backward(stress_pad[4], 0) + backward(stress_pad[5], 1) + forward(stress_pad[2], 2)
    )
    return jnp.stack([velocity_x, velocity_y, velocity_z])


def stress_update(velocity_pad, stress, lame_lambda, shear_modulus):
    strain_x = backward(velocity_pad[0], 0)
    strain_y = backward(velocity_pad[1], 1)
    strain_z = backward(velocity_pad[2], 2)
    stiffness = lame_lambda + 2.0 * shear_modulus
    normal_x = stress[0] + STEP_TIME * (stiffness * strain_x + lame_lambda * (strain_y + strain_z))
    normal_y = stress[1] + STEP_TIME * (stiffness * strain_y + lame_lambda * (strain_x + strain_z))
    normal_z = stress[2] + STEP_TIME * (stiffness * strain_z + lame_lambda * (strain_x + strain_y))
    shear_xy = stress[3] + STEP_TIME * shear_modulus * (
        forward(velocity_pad[0], 1) + forward(velocity_pad[1], 0)
    )
    shear_xz = stress[4] + STEP_TIME * shear_modulus * (
        forward(velocity_pad[0], 2) + forward(velocity_pad[2], 0)
    )
    shear_yz = stress[5] + STEP_TIME * shear_modulus * (
        forward(velocity_pad[1], 2) + forward(velocity_pad[2], 1)
    )
    return jnp.stack([normal_x, normal_y, normal_z, shear_xy, shear_xz, shear_yz])


def build_frames(slip_rate, onsets):
    span = HOP * (STEPS - 1) + TAPS
    offsets = (
        HOP * jnp.arange(STEPS, dtype=jnp.int32)[:, None]
        + jnp.arange(TAPS, dtype=jnp.int32)[None, :]
    )

    def frames_of(row, start):
        return lax.dynamic_slice_in_dim(row, start, span)[offsets]

    return jax.vmap(frames_of)(slip_rate, onsets)


def on_device(
    velocity, stress, buoyancy, lame_lambda, shear_modulus, slip_rate, taps, moment, cells, onsets
):
    frames = build_frames(slip_rate, onsets)
    rates = jnp.einsum("fnk,k->nf", frames, taps, preferred_element_type=jnp.float32)
    local_rate = moment[:, None, :] * rates[None, :, :]
    moment_rate = lax.all_gather(local_rate, ("gx", "gy", "gz"), axis=2, tiled=True)
    width_x, width_y, width_z = buoyancy.shape
    local_x = cells[0] - lax.axis_index("gx") * width_x
    local_y = cells[1] - lax.axis_index("gy") * width_y
    local_z = cells[2] - lax.axis_index("gz") * width_z
    inside = (
        (local_x >= 0)
        & (local_x < width_x)
        & (local_y >= 0)
        & (local_y < width_y)
        & (local_z >= 0)
        & (local_z < width_z)
    )
    local_x = jnp.where(inside, local_x, width_x)
    local_y = jnp.where(inside, local_y, width_y)
    local_z = jnp.where(inside, local_z, width_z)

    def inject(stress_now, step):
        source = lax.dynamic_index_in_dim(moment_rate, step, 1, keepdims=False)
        return stress_now.at[:, local_x, local_y, local_z].add(-STEP_TIME * source, mode="drop")

    def advance(step, carry):
        velocity_now, stress_now = carry
        stress_pad = with_halo(stress_now, (("gx", 1), ("gy", 2), ("gz", 3)), 1)
        velocity_now = velocity_update(stress_pad, velocity_now, buoyancy)
        velocity_pad = with_halo(velocity_now, (("gx", 1), ("gy", 2), ("gz", 3)), 1)
        stress_now = stress_update(velocity_pad, stress_now, lame_lambda, shear_modulus)
        return (velocity_now, inject(stress_now, step))

    velocity_out, stress_out = lax.fori_loop(0, STEPS, advance, (velocity, stress))
    return (velocity_out, stress_out)


def solution(mesh):
    placed = (
        P(None, "gx", "gy", "gz"),
        P(None, "gx", "gy", "gz"),
        P("gx", "gy", "gz"),
        P("gx", "gy", "gz"),
        P("gx", "gy", "gz"),
        P(("gx", "gy", "gz"), None),
        P(),
        P(None, ("gx", "gy", "gz")),
        P(),
        P(("gx", "gy", "gz")),
    )
    return jax.shard_map(
        on_device,
        mesh=mesh,
        in_specs=placed,
        out_specs=(P(None, "gx", "gy", "gz"), P(None, "gx", "gy", "gz")),
        check_vma=False,
    )
```

profile of v0, /device:TPU:30, one launch (start us, length us, event | category | flops | bytes accessed | tf_op | source)
XLA Modules:
  0.0 2108.1 jit_solution(9288432710862921413)
XLA Ops:
  3.7 23.6 %while.17 = (s32[]{:T(128)}, bf16[8,4096]{1,0:T(8,128)(2,1)}, s32[8,2]{0,1:T(2,128)S(1)}, bf16[8,1472]{1,0:T(8,128)(2,1)S(1)}, s32[]{:T(128)}, /*index=5*/s32[]{:T(128)}) while((s32[]{:T(128)}, bf16[8,4096]{1,0:T(8,128)(2,1)}, s32[8,2]{0,1:T(2,128)S(1)}, bf16[8,1472]{1,0:T(8,128)(2,1)S(1)}, s32[]{:T(128)}, /*index=5*/s32[]{:T(128)}) %tuple.89), condition=%wide.while_cond, body=%wide.while_body.sunk | while | flops 2 | bytes 11897 | solution.py:86
  27.7 24.0 %gather_fusion = bf16[8192,8]{1,0:T(8,128)(2,1)S(1)} fusion(bf16[8,1472]{0,1:T(8,128)(2,1)S(1)} %copy.37, s32[8192]{0:T(1024)S(1)} %broadcast_clamp_fusion), kind=kCustom, calls=%fused_computation | custom fusion | bytes 294912 | tf_op jit(solution)/shard_map/vmap()/gather | solution.py:86
  55.0 680.8 %all_gather.3 = f32[6,16,2048]{0,2,1:T(8,128)} all-gather(f32[6,16,8]{0,2,1:T(8,128)S(1)} %broadcast_multiply_fusion), channel_id=1, replica_groups=mesh['gx'=16,'gy'=4,'gz'=4] {'gx','gy','gz'}, dimensions={2}, use_global_device_ids=true | all-gather | bytes 789504 | tf_op jit(solution)/shard_map/all_gather | solution.py:97
  735.8 1368.8 %while.16 = (s32[]{:T(128)}, f32[3,4,8,256]{3,2,1,0:T(8,128)S(1)}, f32[6,4,8,256]{0,3,2,1:T(8,128)}, f32[4,8,256]{2,1,0:T(8,128)S(1)}, f32[4,8,256]{2,1,0:T(8,12...) while((s32[]{:T(128)}, f32[3,4,8,256]{3,2,1,0:T(8,128)S(1)}, ...), condition=%wide.region_2.3_spmd, body=%wide.region_0.2_spmd.sunk | while | flops 2405409 | bytes 10088273 | solution.py:126
  740.7 7.0 collective-permute-start.1
  754.5 8.8 collective-permute-start.3
  785.0 38.0 %collective-permute-start.6 = (f32[3,1,8,256]{3,2,1,0:T(8,128)S(1)}, f32[3,1,8,256]{3,2,1,0:T(8,128)S(1)}, u32[]{:S(2)}, u32[]{:S(2)}) collective-permute-start(f32[3,1,8,256]{3,2,1,0:T(8,128)S(1)} %get-tuple-element.391), channel_id=1, source_target_pairs={{16,0},{32,16},{48,32},{64,48},{80,64},{96,80},{112,96},{128,112},... | collective-permute-start | bytes 73736 | tf_op jit(solution)/shard_map/while/body/eval_jaxpr/ppermute | solution.py:20
  825.0 41.4 %collective-permute-done.7 = f32[3,1,8,256]{3,2,1,0:T(8,128)S(1)} collective-permute-done((f32[3,1,8,256]{3,2,1,0:T(8,128)S(1)}, f32[3,1,8,256]{3,2,1,0:T(8,128)S(1)}, u32[]{:S(2)}, u32[]{:S(2)}) %collective-permute-start.7) | collective-permute-done | bytes 24608 | tf_op jit(solution)/shard_map/while/body/eval_jaxpr/ppermute | solution.py:17
  892.5 14.9 scatter_custom_fusion.5
  975.4 14.9 scatter_custom_fusion.5
  1055.0 14.9 scatter_custom_fusion.5
  1134.6 14.9 scatter_custom_fusion.5
  1214.2 14.9 scatter_custom_fusion.5
  1293.8 14.9 scatter_custom_fusion.5
  1373.4 14.9 scatter_custom_fusion.5
  1452.9 14.9 scatter_custom_fusion.5
  1532.5 14.9 scatter_custom_fusion.5
  1612.1 14.9 scatter_custom_fusion.5
  1691.7 14.9 scatter_custom_fusion.5
  1771.3 14.9 scatter_custom_fusion.5
  1850.9 14.9 scatter_custom_fusion.5
  1930.5 14.9 scatter_custom_fusion.5
  2010.1 14.9 scatter_custom_fusion.5
  2089.7 14.9 scatter_custom_fusion.5
  (894 shorter events, 1064.6 us)
Async XLA Ops:
  738.8 9.1 collective-permute-start
  740.7 11.1 collective-permute-start.1
  751.8 11.5 collective-permute-start.2
  754.5 14.5 collective-permute-start.3
  769.2 10.3 collective-permute-start.4
  775.3 8.6 collective-permute-start.5
  785.0 40.1 %collective-permute-start.6 = (f32[3,1,8,256]{3,2,1,0:T(8,128)S(1)}, f32[3,1,8,256]{3,2,1,0:T(8,128)S(1)}, u32[]{:S(2)}, u32[]{:S(2)}) collective-permute-start(f32[3,1,8,256]{3,2,1,0:T(8,128)S(1)} %get-tuple-element.391), channel_id=1, source_target_pairs={{16,0},{32,16},{48,32},{64,48},{80,64},{96,80},{112,96},{128,112},... | collective-permute-start | bytes 73736 | tf_op jit(solution)/shard_map/while/body/eval_jaxpr/ppermute | solution.py:20
  823.0 43.4 %collective-permute-start.7 = (f32[3,1,8,256]{3,2,1,0:T(8,128)S(1)}, f32[3,1,8,256]{3,2,1,0:T(8,128)S(1)}, u32[]{:S(2)}, u32[]{:S(2)}) collective-permute-start(f32[3,1,8,256]{3,2,1,0:T(8,128)S(1)} %get-tuple-element.392), channel_id=1, source_target_pairs={{0,16},{16,32},{32,48},{48,64},{64,80},{80,96},{96,112},{112,128},... | collective-permute-start | bytes 73736 | tf_op jit(solution)/shard_map/while/body/eval_jaxpr/ppermute | solution.py:17
  875.8 8.5 collective-permute-start.10
  934.6 8.6 collective-permute-start.5
  1014.2 8.6 collective-permute-start.5
  1093.7 8.6 collective-permute-start.5
  1173.3 8.6 collective-permute-start.5
  1252.9 8.6 collective-permute-start.5
  1332.5 8.6 collective-permute-start.5
  1412.1 8.6 collective-permute-start.5
  1491.7 8.6 collective-permute-start.5
  1571.3 8.6 collective-permute-start.5
  1650.9 8.6 collective-permute-start.5
  1730.5 8.6 collective-permute-start.5
  1810.1 8.6 collective-permute-start.5
  1889.7 8.6 collective-permute-start.5
  1969.3 8.6 collective-permute-start.5
  2048.9 8.6 collective-permute-start.5
  (176 other events, 5177.4 us)
where the time goes:
time: 2120 us; the launch traced here: 2110 us
  blocking collectives  681 us (32%)
  waiting for transfers between devices  511 us (24%)
  starting transfers between devices  483 us (23%)
  other arithmetic  278 us (13%)
  local copies, waits for them, and re-layouts  150 us (7%)
    all_gather x1, blocking collectives, on_device(): lax.all_gather(local_rate, ('gx', 'gy', 'gz'), axis=2, tiled=True)  681 us
    ppermute x96, waiting for transfers between devices, with_halo(): lax.ppermute(lax.slice_in_dim(block, block.shape[dim] - width, None, axis...  441 us
    while x144, other arithmetic  250 us
    ppermute x96, starting transfers between devices, with_halo(): lax.ppermute(lax.slice_in_dim(block, block.shape[dim] - width, None, axis...  249 us
    ppermute x96, starting transfers between devices, with_halo(): lax.ppermute(lax.slice_in_dim(block, 0, width, axis=dim), axis, backward)  233 us
    ppermute x96, waiting for transfers between devices, with_halo(): lax.ppermute(lax.slice_in_dim(block, 0, width, axis=dim), axis, backward)  69.7 us
    another operation x16, local copies, waits for them, and re-layouts  46.3 us
    another operation x16, local copies, waits for them, and re-layouts, stress_update(): jnp.stack([normal_x, normal_y, normal_z, shear_xy, shear_xz, shear_yz])  42.5 us
  transfers between devices with their start and end apart: 192, of which 144 were waited for; matrix products, arithmetic and copies ran while one was open for 0% of the time, Pallas kernels for 0%

commit v1 on v0

--- a/solution.py
+++ b/solution.py
@@ -7,6 +7,13 @@
 HOP = 64
 STEPS = 16
 STEP_TIME = 0.25
+
+
+def _save_pages(buf):
+    side_arr = tuple((buf for _ in range(lax.axis_size(("gx", "gy", "gz")))))
+    y1 = jnp.stack(side_arr)
+    mat_out = lax.all_to_all(y1, ("gx", "gy", "gz"), split_axis=0, concat_axis=0)
+    return jnp.concatenate(mat_out, 2)
 
 
 def with_halo(block, sides, width):
@@ -94,7 +101,7 @@
     frames = build_frames(slip_rate, onsets)
     rates = jnp.einsum("fnk,k->nf", frames, taps, preferred_element_type=jnp.float32)
     local_rate = moment[:, None, :] * rates[None, :, :]
-    moment_rate = lax.all_gather(local_rate, ("gx", "gy", "gz"), axis=2, tiled=True)
+    moment_rate = _save_pages(local_rate)
     width_x, width_y, width_z = buoyancy.shape
     local_x = cells[0] - lax.axis_index("gx") * width_x
     local_y = cells[1] - lax.axis_index("gy") * width_y

time: 2120 us -> 1420 us (0.67)
  blocking collectives: 681 us -> 0 us
  local copies, waits for them, and re-layouts: 150 us -> 186 us
  starting transfers between devices: 483 us -> 447 us
    all_gather x1 -> x0, blocking collectives: 681 us -> none  [on_device(): lax.all_gather(local_rate, ('gx', 'gy', 'gz'), axis=2, tiled=True)]
    ppermute x96, starting transfers between devices: 233 us -> 189 us  [with_halo(): lax.ppermute(lax.slice_in_dim(block, 0, width, axis=dim), axis, backward)]
    ppermute x96, waiting for transfers between devices: 441 us -> 401 us  [with_halo(): lax.ppermute(lax.slice_in_dim(block, block.shape[dim] - width, None, axis...]
  transfers between devices with their start and end apart: 192 -> 193, of which waited for: 144 -> 145; matrix products, arithmetic and copies ran while one was open for 0% -> 0% of each run, Pallas kernels for 0% -> 0%
where the time goes in v1:
time: 1420 us; the launch traced here: 1410 us
  waiting for transfers between devices  492 us (35%)
  starting transfers between devices  447 us (31%)
  other arithmetic  282 us (20%)
  local copies, waits for them, and re-layouts  186 us (13%)
    ppermute x96, waiting for transfers between devices, with_halo(): lax.ppermute(lax.slice_in_dim(block, block.shape[dim] - width, None, axis...  401 us
    while x144, other arithmetic  252 us
    ppermute x96, starting transfers between devices, with_halo(): lax.ppermute(lax.slice_in_dim(block, block.shape[dim] - width, None, axis...  243 us
    ppermute x96, starting transfers between devices, with_halo(): lax.ppermute(lax.slice_in_dim(block, 0, width, axis=dim), axis, backward)  189 us
    ppermute x96, waiting for transfers between devices, with_halo(): lax.ppermute(lax.slice_in_dim(block, 0, width, axis=dim), axis, backward)  69.7 us
    another operation x16, local copies, waits for them, and re-layouts  46.3 us
    another operation x16, local copies, waits for them, and re-layouts, stress_update(): jnp.stack([normal_x, normal_y, normal_z, shear_xy, shear_xz, shear_yz])  44.1 us
  transfers between devices with their start and end apart: 193, of which 145 were waited for; matrix products, arithmetic and copies ran while one was open for 0% of the time, Pallas kernels for 0%

profile of v1, /device:TPU:30, one launch (start us, length us, event | category | flops | bytes accessed | tf_op | source)
XLA Modules:
  0.0 1412.2 jit_solution(12417311000694409237)
XLA Ops:
  1.3 23.4 %while.17 = (s32[]{:T(128)}, bf16[8,4096]{1,0:T(8,128)(2,1)}, s32[8,2]{0,1:T(2,128)S(1)}, bf16[8,1472]{1,0:T(8,128)(2,1)S(1)}, s32[]{:T(128)}, /*index=5*/s32[]{:T(128)}) while((s32[]{:T(128)}, bf16[8,4096]{1,0:T(8,128)(2,1)}, s32[8,2]{0,1:T(2,128)S(1)}, bf16[8,1472]{1,0:T(8,128)(2,1)S(1)}, s32[]{:T(128)}, /*index=5*/s32[]{:T(128)}) %tuple.93), condition=%wide.while_cond, body=%wide.while_body.sunk | while | flops 2 | bytes 11889 | solution.py:93
  25.8 24.0 %gather_fusion = bf16[8192,8]{1,0:T(8,128)(2,1)S(1)} fusion(bf16[8,1472]{0,1:T(8,128)(2,1)S(1)} %copy.63, s32[8192]{0:T(1024)S(1)} %broadcast_clamp_fusion), kind=kCustom, calls=%fused_computation | custom fusion | bytes 294912 | tf_op jit(solution)/shard_map/vmap()/gather | solution.py:93
  53.4 5.5 reshape.160
  59.0 14.4 %all-to-all-start = ((f32[256,1,768]{2,1,0:T(1,128)}), f32[256,1,768]{2,1,0:T(1,128)S(1)}, u32[]{:S(2)}, u32[]{:S(2)}) async-start(f32[256,1,768]{2,1,0:T(1,128)} %reshape.160), calls=%async_computation | async-start | bytes 1572864 | tf_op jit(solution)/shard_map/all_to_all | solution.py:15
  76.2 21.1 %all-to-all-done = f32[256,1,768]{2,1,0:T(1,128)S(1)} async-done(((f32[256,1,768]{2,1,0:T(1,128)}), f32[256,1,768]{2,1,0:T(1,128)S(1)}, u32[]{:S(2)}, u32[]{:S(2)}) %all-to-all-start) | async-done | bytes 786464 | tf_op jit(solution)/shard_map/all_to_all | solution.py:15
  104.1 5.8 copy_bitcast_fusion
  110.0 16.9 %copy.66 = f32[6,16,2048]{0,2,1:T(8,128)} copy(f32[6,16,2048]{1,2,0:T(8,128)} %copy_bitcast_fusion) | data formatting | bytes 1572864 | tf_op jit(solution)/shard_map/while | solution.py:133
  126.9 1281.7 %while.16 = (s32[]{:T(128)}, f32[3,4,8,256]{3,2,1,0:T(8,128)S(1)}, f32[6,4,8,256]{0,3,2,1:T(8,128)}, f32[4,8,256]{2,1,0:T(8,128)S(1)}, f32[4,8,256]{2,1,0:T(8,12...) while((s32[]{:T(128)}, f32[3,4,8,256]{3,2,1,0:T(8,128)S(1)}, ...), condition=%wide.region_2.3_spmd, body=%wide.region_0.2_spmd.sunk | while | flops 2405409 | bytes 10088273 | solution.py:133
  195.3 15.0 %scatter_custom_fusion.5 = f32[6,8192]{0,1:T(8,128)} fusion(f32[6,8192]{0,1:T(8,128)} %bitcast.181, s32[2048]{0:T(1024)S(1)} %broadcast_select_fusion.5, f32[6,16,2048]{0,2,1:T(8,128)} %get-tuple-element.489, s32[]{:T(128)} %constant.82.clone.1..sunk, s32[]{:T(128)S(6)} %copy.91, f32[]{:T(128)} %constant.80.clone.1..sunk), kind=kCustom, calls=%fused_computation.3.clone.1 | custom fusion | flops 24576 | bytes 1246212 | tf_op jit(solution)/shard_map/while
  276.5 15.0 %scatter_custom_fusion.5 = f32[6,8192]{0,1:T(8,128)} fusion(f32[6,8192]{0,1:T(8,128)} %bitcast.181, s32[2048]{0:T(1024)S(1)} %broadcast_select_fusion.5, f32[6,16,2048]{0,2,1:T(8,128)} %get-tuple-element.489, s32[]{:T(128)} %constant.82.clone.1..sunk, s32[]{:T(128)S(6)} %copy.91, f32[]{:T(128)} %constant.80.clone.1..sunk), kind=kCustom, calls=%fused_computation.3.clone.1 | custom fusion | flops 24576 | bytes 1246212 | tf_op jit(solution)/shard_map/while
  356.3 15.0 %scatter_custom_fusion.5 = f32[6,8192]{0,1:T(8,128)} fusion(f32[6,8192]{0,1:T(8,128)} %bitcast.181, s32[2048]{0:T(1024)S(1)} %broadcast_select_fusion.5, f32[6,16,2048]{0,2,1:T(8,128)} %get-tuple-element.489, s32[]{:T(128)} %constant.82.clone.1..sunk, s32[]{:T(128)S(6)} %copy.91, f32[]{:T(128)} %constant.80.clone.1..sunk), kind=kCustom, calls=%fused_computation.3.clone.1 | custom fusion | flops 24576 | bytes 1246212 | tf_op jit(solution)/shard_map/while
  436.1 15.0 %scatter_custom_fusion.5 = f32[6,8192]{0,1:T(8,128)} fusion(f32[6,8192]{0,1:T(8,128)} %bitcast.181, s32[2048]{0:T(1024)S(1)} %broadcast_select_fusion.5, f32[6,16,2048]{0,2,1:T(8,128)} %get-tuple-element.489, s32[]{:T(128)} %constant.82.clone.1..sunk, s32[]{:T(128)S(6)} %copy.91, f32[]{:T(128)} %constant.80.clone.1..sunk), kind=kCustom, calls=%fused_computation.3.clone.1 | custom fusion | flops 24576 | bytes 1246212 | tf_op jit(solution)/shard_map/while
  515.9 15.0 %scatter_custom_fusion.5 = f32[6,8192]{0,1:T(8,128)} fusion(f32[6,8192]{0,1:T(8,128)} %bitcast.181, s32[2048]{0:T(1024)S(1)} %broadcast_select_fusion.5, f32[6,16,2048]{0,2,1:T(8,128)} %get-tuple-element.489, s32[]{:T(128)} %constant.82.clone.1..sunk, s32[]{:T(128)S(6)} %copy.91, f32[]{:T(128)} %constant.80.clone.1..sunk), kind=kCustom, calls=%fused_computation.3.clone.1 | custom fusion | flops 24576 | bytes 1246212 | tf_op jit(solution)/shard_map/while
  595.7 15.0 %scatter_custom_fusion.5 = f32[6,8192]{0,1:T(8,128)} fusion(f32[6,8192]{0,1:T(8,128)} %bitcast.181, s32[2048]{0:T(1024)S(1)} %broadcast_select_fusion.5, f32[6,16,2048]{0,2,1:T(8,128)} %get-tuple-element.489, s32[]{:T(128)} %constant.82.clone.1..sunk, s32[]{:T(128)S(6)} %copy.91, f32[]{:T(128)} %constant.80.clone.1..sunk), kind=kCustom, calls=%fused_computation.3.clone.1 | custom fusion | flops 24576 | bytes 1246212 | tf_op jit(solution)/shard_map/while
  675.5 15.0 %scatter_custom_fusion.5 = f32[6,8192]{0,1:T(8,128)} fusion(f32[6,8192]{0,1:T(8,128)} %bitcast.181, s32[2048]{0:T(1024)S(1)} %broadcast_select_fusion.5, f32[6,16,2048]{0,2,1:T(8,128)} %get-tuple-element.489, s32[]{:T(128)} %constant.82.clone.1..sunk, s32[]{:T(128)S(6)} %copy.91, f32[]{:T(128)} %constant.80.clone.1..sunk), kind=kCustom, calls=%fused_computation.3.clone.1 | custom fusion | flops 24576 | bytes 1246212 | tf_op jit(solution)/shard_map/while
  755.3 15.0 %scatter_custom_fusion.5 = f32[6,8192]{0,1:T(8,128)} fusion(f32[6,8192]{0,1:T(8,128)} %bitcast.181, s32[2048]{0:T(1024)S(1)} %broadcast_select_fusion.5, f32[6,16,2048]{0,2,1:T(8,128)} %get-tuple-element.489, s32[]{:T(128)} %constant.82.clone.1..sunk, s32[]{:T(128)S(6)} %copy.91, f32[]{:T(128)} %constant.80.clone.1..sunk), kind=kCustom, calls=%fused_computation.3.clone.1 | custom fusion | flops 24576 | bytes 1246212 | tf_op jit(solution)/shard_map/while
  835.1 15.0 %scatter_custom_fusion.5 = f32[6,8192]{0,1:T(8,128)} fusion(f32[6,8192]{0,1:T(8,128)} %bitcast.181, s32[2048]{0:T(1024)S(1)} %broadcast_select_fusion.5, f32[6,16,2048]{0,2,1:T(8,128)} %get-tuple-element.489, s32[]{:T(128)} %constant.82.clone.1..sunk, s32[]{:T(128)S(6)} %copy.91, f32[]{:T(128)} %constant.80.clone.1..sunk), kind=kCustom, calls=%fused_computation.3.clone.1 | custom fusion | flops 24576 | bytes 1246212 | tf_op jit(solution)/shard_map/while
  914.9 15.0 %scatter_custom_fusion.5 = f32[6,8192]{0,1:T(8,128)} fusion(f32[6,8192]{0,1:T(8,128)} %bitcast.181, s32[2048]{0:T(1024)S(1)} %broadcast_select_fusion.5, f32[6,16,2048]{0,2,1:T(8,128)} %get-tuple-element.489, s32[]{:T(128)} %constant.82.clone.1..sunk, s32[]{:T(128)S(6)} %copy.91, f32[]{:T(128)} %constant.80.clone.1..sunk), kind=kCustom, calls=%fused_computation.3.clone.1 | custom fusion | flops 24576 | bytes 1246212 | tf_op jit(solution)/shard_map/while
  994.7 15.0 %scatter_custom_fusion.5 = f32[6,8192]{0,1:T(8,128)} fusion(f32[6,8192]{0,1:T(8,128)} %bitcast.181, s32[2048]{0:T(1024)S(1)} %broadcast_select_fusion.5, f32[6,16,2048]{0,2,1:T(8,128)} %get-tuple-element.489, s32[]{:T(128)} %constant.82.clone.1..sunk, s32[]{:T(128)S(6)} %copy.91, f32[]{:T(128)} %constant.80.clone.1..sunk), kind=kCustom, calls=%fused_computation.3.clone.1 | custom fusion | flops 24576 | bytes 1246212 | tf_op jit(solution)/shard_map/while
  1074.5 15.0 %scatter_custom_fusion.5 = f32[6,8192]{0,1:T(8,128)} fusion(f32[6,8192]{0,1:T(8,128)} %bitcast.181, s32[2048]{0:T(1024)S(1)} %broadcast_select_fusion.5, f32[6,16,2048]{0,2,1:T(8,128)} %get-tuple-element.489, s32[]{:T(128)} %constant.82.clone.1..sunk, s32[]{:T(128)S(6)} %copy.91, f32[]{:T(128)} %constant.80.clone.1..sunk), kind=kCustom, calls=%fused_computation.3.clone.1 | custom fusion | flops 24576 | bytes 1246212 | tf_op jit(solution)/shard_map/while
  1154.3 15.0 %scatter_custom_fusion.5 = f32[6,8192]{0,1:T(8,128)} fusion(f32[6,8192]{0,1:T(8,128)} %bitcast.181, s32[2048]{0:T(1024)S(1)} %broadcast_select_fusion.5, f32[6,16,2048]{0,2,1:T(8,128)} %get-tuple-element.489, s32[]{:T(128)} %constant.82.clone.1..sunk, s32[]{:T(128)S(6)} %copy.91, f32[]{:T(128)} %constant.80.clone.1..sunk), kind=kCustom, calls=%fused_computation.3.clone.1 | custom fusion | flops 24576 | bytes 1246212 | tf_op jit(solution)/shard_map/while
  1234.1 15.0 %scatter_custom_fusion.5 = f32[6,8192]{0,1:T(8,128)} fusion(f32[6,8192]{0,1:T(8,128)} %bitcast.181, s32[2048]{0:T(1024)S(1)} %broadcast_select_fusion.5, f32[6,16,2048]{0,2,1:T(8,128)} %get-tuple-element.489, s32[]{:T(128)} %constant.82.clone.1..sunk, s32[]{:T(128)S(6)} %copy.91, f32[]{:T(128)} %constant.80.clone.1..sunk), kind=kCustom, calls=%fused_computation.3.clone.1 | custom fusion | flops 24576 | bytes 1246212 | tf_op jit(solution)/shard_map/while
  1313.9 15.0 %scatter_custom_fusion.5 = f32[6,8192]{0,1:T(8,128)} fusion(f32[6,8192]{0,1:T(8,128)} %bitcast.181, s32[2048]{0:T(1024)S(1)} %broadcast_select_fusion.5, f32[6,16,2048]{0,2,1:T(8,128)} %get-tuple-element.489, s32[]{:T(128)} %constant.82.clone.1..sunk, s32[]{:T(128)S(6)} %copy.91, f32[]{:T(128)} %constant.80.clone.1..sunk), kind=kCustom, calls=%fused_computation.3.clone.1 | custom fusion | flops 24576 | bytes 1246212 | tf_op jit(solution)/shard_map/while
  1393.7 15.0 %scatter_custom_fusion.5 = f32[6,8192]{0,1:T(8,128)} fusion(f32[6,8192]{0,1:T(8,128)} %bitcast.181, s32[2048]{0:T(1024)S(1)} %broadcast_select_fusion.5, f32[6,16,2048]{0,2,1:T(8,128)} %get-tuple-element.489, s32[]{:T(128)} %constant.82.clone.1..sunk, s32[]{:T(128)S(6)} %copy.91, f32[]{:T(128)} %constant.80.clone.1..sunk), kind=kCustom, calls=%fused_computation.3.clone.1 | custom fusion | flops 24576 | bytes 1246212 | tf_op jit(solution)/shard_map/while
  (906 shorter events, 1079.2 us)
Async XLA Ops:
  59.0 38.3 %all-to-all-start = ((f32[256,1,768]{2,1,0:T(1,128)}), f32[256,1,768]{2,1,0:T(1,128)S(1)}, u32[]{:S(2)}, u32[]{:S(2)}) async-start(f32[256,1,768]{2,1,0:T(1,128)} %reshape.160), calls=%async_computation | async-start | bytes 1572864 | tf_op jit(solution)/shard_map/all_to_all | solution.py:15
  131.8 8.1 collective-permute-start.1
  152.9 8.6 collective-permute-start.5
  235.6 8.6 collective-permute-start.5
  296.3 8.1 collective-permute-start.1
  315.4 8.6 collective-permute-start.5
  376.1 8.1 collective-permute-start.1
  395.2 8.6 collective-permute-start.5
  455.9 8.1 collective-permute-start.1
  475.0 8.6 collective-permute-start.5
  535.7 8.1 collective-permute-start.1
  554.8 8.6 collective-permute-start.5
  615.5 8.1 collective-permute-start.1
  634.6 8.6 collective-permute-start.5
  695.3 8.1 collective-permute-start.1
  714.4 8.6 collective-permute-start.5
  794.2 8.6 collective-permute-start.5
  874.0 8.6 collective-permute-start.5
  953.8 8.6 collective-permute-start.5
  1033.6 8.6 collective-permute-start.5
  1113.4 8.6 collective-permute-start.5
  1193.2 8.6 collective-permute-start.5
  1273.0 8.6 collective-permute-start.5
  1352.8 8.6 collective-permute-start.5
  (179 other events, 1224.1 us)
